TPU v7x, 512 devices: a whole 4x4x16 slice. The times are simulated.
512 devices in a mesh: blk: 32 (over z, core), col: 16 (over y, x).
Axes of the slice: x: 4, y: 4, z: 16, core: 2. Of those that a mesh axis runs over, the one named last changes fastest.
Arguments:
- density: float32 [96, 7, 256, 256], P('blk', None, 'col'), as said below
- band_widths: int32 [96], P('blk'), may hold values from 1 to 3, as said below
Outputs:
- purified: float32 [96, 7, 256, 256], P('blk', None, 'col')
Inputs may be any that keep to these rules, and one draw needn't show every extreme that they name: `band_widths`: each block row keeps between 1 and 3 blocks on each side; 3 is reached in every draw. `density`: diagonal entries of the diagonal blocks lie between 0.05 and 0.95, all other entries are small.
All inputs are finite; a program needn't handle non-finite values.
Results may differ from a plain program's by a relative error of at most 0.00013.
Values sent between devices are 32-bit elements; how exact they have to be, the bound alone decides.
No kernel may reach another device: no remote copies, remote signals or barrier semaphores. Data moves between devices by JAX's collectives and lax.ppermute only.
A program may use at most 64 MiB of HBM per device.

v0:
```python
import jax
import jax.numpy as jnp
from jax import lax
from jax.sharding import PartitionSpec as P

W = 3


def send(cells, shift):
    count = lax.axis_size("blk")
    return lax.ppermute(cells, "blk", [(i, (i + shift) % count) for i in range(count)])


def halo_pieces(cells):
    rows = cells.shape[0]
    tail = [cells[rows - W + k, W - k :] for k in range(W)]
    head = [cells[k, : 2 * W - k] for k in range(W)]
    return (tail, head)


def extend(right):
    tail, head = halo_pieces(right)
    from_left = send(jnp.concatenate(tail, axis=0), 1)
    from_right = send(jnp.concatenate(head, axis=0), -1)
    zero = jnp.zeros((1,) + right.shape[2:], right.dtype)
    rows = []
    start = 0
    for k in range(W):
        width = 2 * W + 1 - (W - k)
        piece = from_left[start : start + width]
        start += width
        rows.append(
            jnp.concatenate([jnp.broadcast_to(zero, (W - k,) + right.shape[2:]), piece], axis=0)
        )
    left = jnp.stack(rows)
    rows = []
    start = 0
    for k in range(W):
        width = 2 * W - k
        piece = from_right[start : start + width]
        start += width
        rows.append(
            jnp.concatenate([piece, jnp.broadcast_to(zero, (k + 1,) + right.shape[2:])], axis=0)
        )
    right_rows = jnp.stack(rows)
    return jnp.concatenate([left, right, right_rows], axis=0)


def contract(extended, shard_rows, keep=None):
    local_rows = shard_rows.shape[0]
    span = 2 * W + 1
    zeros = jnp.zeros_like(extended[:local_rows, :1])
    shifted = []
    for inner_band in range(span):
        window = extended[inner_band : inner_band + local_rows]
        shift = inner_band - W
        if shift > 0:
            window = jnp.concatenate([zeros] * shift + [window[:, : span - shift]], axis=1)
        elif shift < 0:
            window = jnp.concatenate([window[:, -shift:]] + [zeros] * -shift, axis=1)
        shifted.append(window)
    stacked = jnp.stack(shifted, axis=3)
    if keep is not None:
        shard_rows = shard_rows * keep
    return jnp.einsum("ibcas,iasr->ibcr", stacked, shard_rows, precision=lax.Precision.HIGH)


def on_device(density, band_widths):
    offsets = jnp.abs(jnp.arange(2 * W + 1, dtype=jnp.int32) - W)
    pattern = (offsets[None, :] <= band_widths[:, None]).astype(jnp.float32)[:, :, None, None]
    current = density * pattern
    for purify_step in range(2):
        if purify_step == 0:
            gathered, keep = (lax.all_gather(density, "col", axis=2, tiled=True), pattern)
        else:
            gathered, keep = (lax.all_gather(current, "col", axis=2, tiled=True), None)
        square = contract(extend(current), gathered, keep) * pattern
        third_power = contract(extend(square), gathered, keep) * pattern
        current = 3.0 * square - 2.0 * third_power
    return current


def solution(mesh):
    in_specs = (P("blk", None, "col", None), P("blk"))
    out_specs = P("blk", None, "col", None)
    return jax.shard_map(
        on_device, mesh=mesh, in_specs=in_specs, out_specs=out_specs, check_vma=False
    )
```

profile of v0, /device:TPU:97, one launch (start us, length us, event | category | flops | bytes accessed | tf_op | source)
XLA Modules:
  0.0 198.5 jit_solution(10707903417032842990)
XLA Ops:
  6.5 0.0 all-gather.3.cloned.1.call-start
  6.5 0.7 all-gather.3.cloned.1.call-update
  7.3 0.0 all-gather.5.cloned.1.call-start
  7.3 0.7 compare_convert_fusion
  8.0 1.1 broadcast_multiply_fusion
  9.2 0.0 copy-start.2
  9.2 3.4 %collective-permute-start = (f32[15,16,256]{2,1,0:T(8,128)S(1)}, f32[15,16,256]{2,1,0:T(8,128)S(1)}, u32[]{:S(2)}, u32[]{:S(2)}) collective-permute-start(f32[15,16,256]{2,1,0:T(8,128)S(1)} %pad_maximum_fusion), channel_id=1, source_target_pairs={{0,16},{16,32},{32,48},{48,64},{64,80},{80,96},{96,112},{112,128},... | collective-permute-start | bytes 737288 | tf_op jit(solution)/shard_map/ppermute | solution.py:11
  12.7 0.0 collective-permute-start.1
  12.7 3.1 %collective-permute-done = f32[15,16,256]{2,1,0:T(8,128)S(1)} collective-permute-done((f32[15,16,256]{2,1,0:T(8,128)S(1)}, f32[15,16,256]{2,1,0:T(8,128)S(1)}, u32[]{:S(2)}, u32[]{:S(2)}) %collective-permute-start) | collective-permute-done | bytes 245792 | tf_op jit(solution)/shard_map/ppermute | solution.py:11
  15.8 3.7 %collective-permute-done.1 = f32[15,16,256]{2,1,0:T(8,128)S(1)} collective-permute-done((f32[15,16,256]{2,1,0:T(8,128)S(1)}, f32[15,16,256]{2,1,0:T(8,128)S(1)}, u32[]{:S(2)}, u32[]{:S(2)}) %collective-permute-start.1) | collective-permute-done | bytes 245792 | tf_op jit(solution)/shard_map/ppermute | solution.py:11
  19.7 0.0 copy-done.2
  19.7 0.1 fusion.84
  19.8 0.0 copy-done.1
  19.8 0.1 bitcast_dynamic-update-slice_fusion
  20.0 66.8 %all-gather.3.cloned.1.call-done = f32[3,7,256,256]{3,2,1,0:T(8,128)} async-done(((f32[3,7,16,256]{3,2,1,0:T(8,128)}), f32[3,7,256,256]{3,2,1,0:T(8,128)}) %all-gather.3.cloned.1.call-update) | async-done | bytes 5505040 | tf_op jit(solution)/shard_map/all_gather | solution.py:74
  86.8 4.4 %fusion.16 = f32[3,7,16,256]{3,2,1,0:T(8,128)S(1)} fusion(f32[3,7,16,7,256]{4,2,3,1,0:T(8,128)S(1)} %fusion.68, f32[3,7,256,256]{3,2,1,0:T(8,128)} %all-gather.3.cloned.1.call-done, f32[3,7]{1,0:T(4,128)S(1)} %compare_convert_fusion), kind=kOutput, calls=%fused_computation.15 | convolution fusion | flops 926306304 | bytes 8257620 | tf_op jit(solution)/shard_map/ibcas,iasr->ibcr/dot_general | solution.py:65
  91.2 0.0 slice-start.1
  91.3 3.1 %collective-permute-start.2 = (f32[15,16,256]{2,1,0:T(8,128)S(1)}, f32[15,16,256]{2,1,0:T(8,128)S(1)}, u32[]{:S(2)}, u32[]{:S(2)}) collective-permute-start(f32[15,16,256]{2,1,0:T(8,128)S(1)} %pad_maximum_fusion.2), channel_id=1, source_target_pairs={{0,16},{16,32},{32,48},{48,64},{64,80},{80,96},{96,112},{112,128},... | collective-permute-start | bytes 737288 | tf_op jit(solution)/shard_map/ppermute | solution.py:11
  94.4 0.0 collective-permute-start.3
  94.4 3.1 %collective-permute-done.2 = f32[15,16,256]{2,1,0:T(8,128)S(1)} collective-permute-done((f32[15,16,256]{2,1,0:T(8,128)S(1)}, f32[15,16,256]{2,1,0:T(8,128)S(1)}, u32[]{:S(2)}, u32[]{:S(2)}) %collective-permute-start.2) | collective-permute-done | bytes 245792 | tf_op jit(solution)/shard_map/ppermute | solution.py:11
  97.7 3.5 %collective-permute-done.3 = f32[15,16,256]{2,1,0:T(8,128)S(1)} collective-permute-done((f32[15,16,256]{2,1,0:T(8,128)S(1)}, f32[15,16,256]{2,1,0:T(8,128)S(1)}, u32[]{:S(2)}, u32[]{:S(2)}) %collective-permute-start.3) | collective-permute-done | bytes 245792 | tf_op jit(solution)/shard_map/ppermute | solution.py:11
  101.3 0.1 fusion.83
  101.4 0.0 slice-done
  101.5 0.0 slice-done.1
  101.5 1.7 fusion.2
  103.2 0.8 fusion.80
  104.0 0.0 all-gather.5.cloned.1.call-update
  104.0 0.9 slice_bitcast_fusion.18
  105.0 1.0 slice_bitcast_fusion.10
  106.0 1.0 slice_bitcast_fusion.2
  106.9 0.2 collective-permute-start.4
  107.2 0.3 collective-permute-start.5
  107.5 2.8 %collective-permute-done.4 = f32[15,16,256]{2,1,0:T(8,128)S(1)} collective-permute-done((f32[15,16,256]{2,1,0:T(8,128)S(1)}, f32[15,16,256]{2,1,0:T(8,128)S(1)}, u32[]{:S(2)}, u32[]{:S(2)}) %collective-permute-start.4) | collective-permute-done | bytes 245792 | tf_op jit(solution)/shard_map/ppermute | solution.py:11
  110.3 3.7 %collective-permute-done.5 = f32[15,16,256]{2,1,0:T(8,128)S(1)} collective-permute-done((f32[15,16,256]{2,1,0:T(8,128)S(1)}, f32[15,16,256]{2,1,0:T(8,128)S(1)}, u32[]{:S(2)}, u32[]{:S(2)}) %collective-permute-start.5) | collective-permute-done | bytes 245792 | tf_op jit(solution)/shard_map/ppermute | solution.py:11
  114.2 0.0 copy-done
  114.2 0.1 fusion.82
  114.4 59.8 %all-gather.5.cloned.1.call-done = f32[3,7,256,256]{3,2,1,0:T(8,128)} async-done(((f32[3,7,16,256]{3,2,1,0:T(8,128)}), f32[3,7,256,256]{3,2,1,0:T(8,128)}) %all-gather.5.cloned.1.call-update) | async-done | bytes 5505040 | tf_op jit(solution)/shard_map/all_gather | solution.py:76
  174.2 4.4 %fusion.6 = f32[3,7,16,256,1]{3,2,0,1,4:T(8,128)S(1)} fusion(f32[3,7,16,7,256]{4,2,1,0,3:T(8,128)S(1)} %fusion.32, f32[3,7,256,256]{3,2,1,0:T(8,128)} %all-gather.5.cloned.1.call-done), kind=kOutput, calls=%fused_computation.6 | convolution fusion | flops 924844032 | bytes 8257536 | tf_op jit(solution)/shard_map/ibcas,iasr->ibcr/dot_general | solution.py:65
  178.7 0.1 bitcast_multiply_fusion.1
  178.8 0.0 slice-start.3
  178.9 3.1 %collective-permute-start.6 = (f32[15,16,256]{2,1,0:T(8,128)S(1)}, f32[15,16,256]{2,1,0:T(8,128)S(1)}, u32[]{:S(2)}, u32[]{:S(2)}) collective-permute-start(f32[15,16,256]{2,1,0:T(8,128)S(1)} %pad_maximum_fusion.6), channel_id=1, source_target_pairs={{0,16},{16,32},{32,48},{48,64},{64,80},{80,96},{96,112},{112,128},... | collective-permute-start | bytes 737288 | tf_op jit(solution)/shard_map/ppermute | solution.py:11
  181.9 0.0 collective-permute-start.7
  182.0 3.1 %collective-permute-done.6 = f32[15,16,256]{2,1,0:T(8,128)S(1)} collective-permute-done((f32[15,16,256]{2,1,0:T(8,128)S(1)}, f32[15,16,256]{2,1,0:T(8,128)S(1)}, u32[]{:S(2)}, u32[]{:S(2)}) %collective-permute-start.6) | collective-permute-done | bytes 245792 | tf_op jit(solution)/shard_map/ppermute | solution.py:11
  185.2 0.1 bitcast_dynamic-update-slice_fusion.1
  185.3 3.4 %collective-permute-done.7 = f32[15,16,256]{2,1,0:T(8,128)S(1)} collective-permute-done((f32[15,16,256]{2,1,0:T(8,128)S(1)}, f32[15,16,256]{2,1,0:T(8,128)S(1)}, u32[]{:S(2)}, u32[]{:S(2)}) %collective-permute-start.7) | collective-permute-done | bytes 245792 | tf_op jit(solution)/shard_map/ppermute | solution.py:11
  188.8 0.1 fusion.81
  189.0 1.8 fusion.4
  190.8 0.9 fusion.78
  (90 shorter events, 1.2 us)
Async XLA Ops:
  6.5 80.2 %all-gather.3.cloned.1.call-start = ((), (), s32[]{:S(2)}) async-start(), calls=%async_computation | async-start | bytes 5849088 | tf_op jit(solution)/shard_map/all_gather | solution.py:74
  7.3 167.0 %all-gather.5.cloned.1.call-start = ((), (), s32[]{:S(2)}) async-start(), calls=%async_computation.1 | async-start | bytes 5849088 | tf_op jit(solution)/shard_map/all_gather | solution.py:76
  9.2 10.5 %copy-start.2 = (pred[7]{0:T(512)(128)(4,1)S(1)}, pred[7]{0:T(512)(128)(4,1)}, u32[]{:S(2)}) copy-start(pred[7]{0:T(512)(128)(4,1)} %constant.7.clone.1) | copy-start | bytes 25
  9.2 6.6 %collective-permute-start = (f32[15,16,256]{2,1,0:T(8,128)S(1)}, f32[15,16,256]{2,1,0:T(8,128)S(1)}, u32[]{:S(2)}, u32[]{:S(2)}) collective-permute-start(f32[15,16,256]{2,1,0:T(8,128)S(1)} %pad_maximum_fusion), channel_id=1, source_target_pairs={{0,16},{16,32},{32,48},{48,64},{64,80},{80,96},{96,112},{112,128},... | collective-permute-start | bytes 737288 | tf_op jit(solution)/shard_map/ppermute | solution.py:11
  12.6 7.1 %copy-start.1 = (f32[3,7,16,256]{3,2,1,0:T(8,128)S(1)}, f32[3,7,16,256]{3,2,1,0:T(8,128)}, u32[]{:S(2)}) copy-start(f32[3,7,16,256]{3,2,1,0:T(8,128)} %param.2) | copy-start | bytes 1032196
  12.7 6.8 %collective-permute-start.1 = (f32[15,16,256]{2,1,0:T(8,128)S(1)}, f32[15,16,256]{2,1,0:T(8,128)S(1)}, u32[]{:S(2)}, u32[]{:S(2)}) collective-permute-start(f32[15,16,256]{2,1,0:T(8,128)S(1)} %pad_maximum_fusion.1), channel_id=1, source_target_pairs={{0,496},{16,0},{32,16},{48,32},{64,48},{80,64},{96,80},{112,96},{1... | collective-permute-start | bytes 737288 | tf_op jit(solution)/shard_map/ppermute | solution.py:11
  86.8 14.7 %slice-start = ((s8[5505024]{0:T(1024)(128)(4,1)}), s8[4194304]{0:T(1024)(128)(4,1)S(1)}, s32[]{:S(2)}) async-start(s8[5505024]{0:T(1024)(128)(4,1)} %bitcast.255), calls=%async_computation.2 | async-start | bytes 8388608
  91.2 10.2 %slice-start.1 = ((s8[5505024]{0:T(1024)(128)(4,1)}), s8[1310720]{0:T(1024)(128)(4,1)S(1)}, s32[]{:S(2)}) async-start(s8[5505024]{0:T(1024)(128)(4,1)} %bitcast.255), calls=%async_computation.3 | async-start | bytes 2621440
  91.3 6.2 %collective-permute-start.2 = (f32[15,16,256]{2,1,0:T(8,128)S(1)}, f32[15,16,256]{2,1,0:T(8,128)S(1)}, u32[]{:S(2)}, u32[]{:S(2)}) collective-permute-start(f32[15,16,256]{2,1,0:T(8,128)S(1)} %pad_maximum_fusion.2), channel_id=1, source_target_pairs={{0,16},{16,32},{32,48},{48,64},{64,80},{80,96},{96,112},{112,128},... | collective-permute-start | bytes 737288 | tf_op jit(solution)/shard_map/ppermute | solution.py:11
  94.4 6.8 %collective-permute-start.3 = (f32[15,16,256]{2,1,0:T(8,128)S(1)}, f32[15,16,256]{2,1,0:T(8,128)S(1)}, u32[]{:S(2)}, u32[]{:S(2)}) collective-permute-start(f32[15,16,256]{2,1,0:T(8,128)S(1)} %pad_maximum_fusion.3), channel_id=1, source_target_pairs={{0,496},{16,0},{32,16},{48,32},{64,48},{80,64},{96,80},{112,96},{1... | collective-permute-start | bytes 737288 | tf_op jit(solution)/shard_map/ppermute | solution.py:11
  104.0 10.1 %copy-start = (f32[3,7,16,256]{3,2,1,0:T(8,128)S(1)}, f32[3,7,16,256]{3,2,1,0:T(8,128)}, u32[]{:S(2)}) copy-start(f32[3,7,16,256]{3,2,1,0:T(8,128)} %fusion.80) | copy-start | bytes 1032196
  106.9 3.4 %collective-permute-start.4 = (f32[15,16,256]{2,1,0:T(8,128)S(1)}, f32[15,16,256]{2,1,0:T(8,128)S(1)}, u32[]{:S(2)}, u32[]{:S(2)}) collective-permute-start(f32[15,16,256]{2,1,0:T(8,128)S(1)} %pad_maximum_fusion.4), channel_id=1, source_target_pairs={{0,16},{16,32},{32,48},{48,64},{64,80},{80,96},{96,112},{112,128},... | collective-permute-start | bytes 737288 | tf_op jit(solution)/shard_map/ppermute | solution.py:11
  107.2 6.8 %collective-permute-start.5 = (f32[15,16,256]{2,1,0:T(8,128)S(1)}, f32[15,16,256]{2,1,0:T(8,128)S(1)}, u32[]{:S(2)}, u32[]{:S(2)}) collective-permute-start(f32[15,16,256]{2,1,0:T(8,128)S(1)} %pad_maximum_fusion.5), channel_id=1, source_target_pairs={{0,496},{16,0},{32,16},{48,32},{64,48},{80,64},{96,80},{112,96},{1... | collective-permute-start | bytes 737288 | tf_op jit(solution)/shard_map/ppermute | solution.py:11
  174.2 14.8 %slice-start.2 = ((s8[5505024]{0:T(1024)(128)(4,1)}), s8[4194304]{0:T(1024)(128)(4,1)S(1)}, s32[]{:S(2)}) async-start(s8[5505024]{0:T(1024)(128)(4,1)} %bitcast.257), calls=%async_computation.4 | async-start | bytes 8388608
  178.8 10.3 %slice-start.3 = ((s8[5505024]{0:T(1024)(128)(4,1)}), s8[1310720]{0:T(1024)(128)(4,1)S(1)}, s32[]{:S(2)}) async-start(s8[5505024]{0:T(1024)(128)(4,1)} %bitcast.257), calls=%async_computation.5 | async-start | bytes 2621440
  178.9 6.2 %collective-permute-start.6 = (f32[15,16,256]{2,1,0:T(8,128)S(1)}, f32[15,16,256]{2,1,0:T(8,128)S(1)}, u32[]{:S(2)}, u32[]{:S(2)}) collective-permute-start(f32[15,16,256]{2,1,0:T(8,128)S(1)} %pad_maximum_fusion.6), channel_id=1, source_target_pairs={{0,16},{16,32},{32,48},{48,64},{64,80},{80,96},{96,112},{112,128},... | collective-permute-start | bytes 737288 | tf_op jit(solution)/shard_map/ppermute | solution.py:11
  181.9 6.8 %collective-permute-start.7 = (f32[15,16,256]{2,1,0:T(8,128)S(1)}, f32[15,16,256]{2,1,0:T(8,128)S(1)}, u32[]{:S(2)}, u32[]{:S(2)}) collective-permute-start(f32[15,16,256]{2,1,0:T(8,128)S(1)} %pad_maximum_fusion.7), channel_id=1, source_target_pairs={{0,496},{16,0},{32,16},{48,32},{64,48},{80,64},{96,80},{112,96},{1... | collective-permute-start | bytes 737288 | tf_op jit(solution)/shard_map/ppermute | solution.py:11
Sparse Core Ops, SparseCore 0:
  10.4 76.3 all-gather.2
  104.2 70.0 all-gather.4
where the time goes:
time: 199 us; the launch traced here: 198 us
  waiting for transfers between devices  154 us (77%)
  between operations  14.1 us (7%)
  matrix products  12.3 us (6%)
  starting transfers between devices  10.2 us (5%)
  other arithmetic  4.81 us (2%)
  local copies, waits for them, and re-layouts  3.36 us (2%)
    all_gather x1, waiting for transfers between devices, on_device(): lax.all_gather(density, 'col', axis=2, tiled=True)  66.8 us
    all_gather x1, waiting for transfers between devices, on_device(): gathered, keep = (lax.all_gather(current, 'col', axis=2, tiled=True), None)  59.8 us
    ppermute x8, waiting for transfers between devices, send(): lax.ppermute(cells, 'blk', [(i, (i + shift) % count) for i in range(count)])  26.4 us
    dot_general x4, matrix products, contract(): jnp.einsum('ibcas,iasr->ibcr', stacked, shard_rows, precision=lax.Precisi...  12.3 us
    ppermute x8, starting transfers between devices, send(): lax.ppermute(cells, 'blk', [(i, (i + shift) % count) for i in range(count)])  10.1 us
  transfers between devices with their start and end apart: 10, of which 10 were waited for; matrix products, arithmetic and copies ran while one was open for 3% of the time, Pallas kernels for 0%

commit v1 on v0

--- a/solution.py
+++ b/solution.py
@@ -4,6 +4,11 @@
 from jax.sharding import PartitionSpec as P
 
 W = 3
+
+
+def gather_from_all(shard, axis, dim):
+    copies = jnp.concatenate([shard] * lax.axis_size(axis), axis=dim)
+    return lax.all_to_all(copies, axis, dim, dim, tiled=True)
 
 
 def send(cells, shift):
@@ -73,7 +78,7 @@
         if purify_step == 0:
             gathered, keep = (lax.all_gather(density, "col", axis=2, tiled=True), pattern)
         else:
-            gathered, keep = (lax.all_gather(current, "col", axis=2, tiled=True), None)
+            gathered, keep = (gather_from_all(current, "col", 2), None)
         square = contract(extend(current), gathered, keep) * pattern
         third_power = contract(extend(square), gathered, keep) * pattern
         current = 3.0 * square - 2.0 * third_power

time: 199 us -> 239 us (1.20)
  the two profiles are of different devices: /device:TPU:97 before, /device:TPU:1 now
where the time goes in v1:
time: 239 us
  waiting for transfers between devices  175 us (73%)
  starting transfers between devices  21 us (9%)
  matrix products  18 us (8%)
  between operations  14.2 us (6%)
  local copies, waits for them, and re-layouts  6.77 us (3%)
  other arithmetic  4.09 us (2%)
    all_to_all x1, waiting for transfers between devices, gather_from_all(): return lax.all_to_all(copies, axis, dim, dim, tiled=True)  85.5 us
    all_gather x1, waiting for transfers between devices, on_device(): lax.all_gather(density, 'col', axis=2, tiled=True)  70.4 us
    dot_general x4, matrix products, contract(): jnp.einsum('ibcas,iasr->ibcr', stacked, shard_rows, precision=lax.Precisi...  18 us
    ppermute x8, waiting for transfers between devices, send(): lax.ppermute(cells, 'blk', [(i, (i + shift) % count) for i in range(count)])  18 us
    ppermute x8, starting transfers between devices, send(): lax.ppermute(cells, 'blk', [(i, (i + shift) % count) for i in range(count)])  15.9 us
    concatenate x2, local copies, waits for them, and re-layouts, gather_from_all(): copies = jnp.concatenate([shard] * lax.axis_size(axis), axis=dim)  5.89 us
    all_to_all x1, starting transfers between devices, gather_from_all(): return lax.all_to_all(copies, axis, dim, dim, tiled=True)  5.03 us
  transfers between devices with their start and end apart: 10, of which 10 were waited for; matrix products, arithmetic and copies ran while one was open for 1% of the time, Pallas kernels for 0%

profile of v1, /device:TPU:1, one launch (start us, length us, event | category | flops | bytes accessed | tf_op | source)
XLA Modules:
  0.0 238.7 jit_solution(17688081627496066878)
XLA Ops:
  6.5 0.0 all-gather.2.cloned.1.call-start
  6.5 0.7 all-gather.2.cloned.1.call-update
  7.3 0.7 compare_convert_fusion
  8.0 1.1 broadcast_multiply_fusion
  9.1 0.0 copy-start.1
  9.2 3.0 %collective-permute-start = (f32[15,16,256]{2,1,0:T(8,128)S(1)}, f32[15,16,256]{2,1,0:T(8,128)S(1)}, u32[]{:S(2)}, u32[]{:S(2)}) collective-permute-start(f32[15,16,256]{2,1,0:T(8,128)S(1)} %pad_maximum_fusion), channel_id=1, source_target_pairs={{0,16},{16,32},{32,48},{48,64},{64,80},{80,96},{96,112},{112,128},... | collective-permute-start | bytes 737288 | tf_op jit(solution)/shard_map/ppermute | solution.py:16
  12.2 0.0 copy-start
  12.2 3.9 %collective-permute-start.1 = (f32[15,16,256]{2,1,0:T(8,128)S(1)}, f32[15,16,256]{2,1,0:T(8,128)S(1)}, u32[]{:S(2)}, u32[]{:S(2)}) collective-permute-start(f32[15,16,256]{2,1,0:T(8,128)S(1)} %pad_maximum_fusion.1), channel_id=1, source_target_pairs={{0,496},{16,0},{32,16},{48,32},{64,48},{80,64},{96,80},{112,96},{1... | collective-permute-start | bytes 737288 | tf_op jit(solution)/shard_map/ppermute | solution.py:16
  16.1 0.9 collective-permute-done
  17.1 0.8 collective-permute-done.1
  18.0 0.0 copy-done.1
  18.0 0.1 fusion.84
  18.1 0.0 copy-done
  18.1 0.1 bitcast_dynamic-update-slice_fusion
  18.3 70.4 %all-gather.2.cloned.1.call-done = f32[3,7,256,256]{3,2,1,0:T(8,128)} async-done(((f32[3,7,16,256]{3,2,1,0:T(8,128)}), f32[3,7,256,256]{3,2,1,0:T(8,128)}) %all-gather.2.cloned.1.call-update) | async-done | bytes 5505040 | tf_op jit(solution)/shard_map/all_gather | solution.py:79
  88.7 0.0 slice-start
  88.7 4.4 %fusion.16 = f32[3,7,16,256]{3,2,1,0:T(8,128)S(1)} fusion(f32[3,7,16,7,256]{4,2,3,1,0:T(8,128)S(1)} %fusion.68, f32[3,7,256,256]{3,2,1,0:T(8,128)} %all-gather.2.cloned.1.call-done, f32[3,7]{1,0:T(4,128)S(1)} %compare_convert_fusion), kind=kOutput, calls=%fused_computation.15 | convolution fusion | flops 926306304 | bytes 8257620 | tf_op jit(solution)/shard_map/ibcas,iasr->ibcr/dot_general | solution.py:70
  93.1 0.0 slice-start.1
  93.2 1.8 collective-permute-start.2
  95.1 0.0 collective-permute-start.3
  95.1 3.1 %collective-permute-done.2 = f32[15,16,256]{2,1,0:T(8,128)S(1)} collective-permute-done((f32[15,16,256]{2,1,0:T(8,128)S(1)}, f32[15,16,256]{2,1,0:T(8,128)S(1)}, u32[]{:S(2)}, u32[]{:S(2)}) %collective-permute-start.2) | collective-permute-done | bytes 245792 | tf_op jit(solution)/shard_map/ppermute | solution.py:16
  98.4 2.5 %collective-permute-done.3 = f32[15,16,256]{2,1,0:T(8,128)S(1)} collective-permute-done((f32[15,16,256]{2,1,0:T(8,128)S(1)}, f32[15,16,256]{2,1,0:T(8,128)S(1)}, u32[]{:S(2)}, u32[]{:S(2)}) %collective-permute-start.3) | collective-permute-done | bytes 245792 | tf_op jit(solution)/shard_map/ppermute | solution.py:16
  100.9 0.1 fusion.83
  101.1 0.0 slice-done
  101.1 0.0 slice-done.1
  101.1 1.7 fusion.2
  102.8 0.1 constant_dynamic-update-slice_fusion.15
  103.5 5.9 %copy.19 = f32[3,7,256,256]{3,1,0,2:T(8,128)} copy(f32[3,7,256,256]{3,2,1,0:T(8,128)S(1)} %constant_dynamic-update-slice_fusion) | data formatting | bytes 11010048 | tf_op jit(solution)/shard_map/concatenate | solution.py:10
  109.3 5.0 %all-to-all-start = ((f32[3,7,256,256]{3,1,0,2:T(8,128)}), f32[3,7,256,256]{3,1,0,2:T(8,128)}, u32[]{:S(2)}, u32[]{:S(2)}) async-start(f32[3,7,256,256]{3,1,0,2:T(8,128)} %copy.19), calls=%async_computation | async-start | bytes 12582912 | tf_op jit(solution)/shard_map/all_to_all | solution.py:11
  114.5 0.3 collective-permute-start.4
  114.8 0.6 collective-permute-start.5
  115.5 2.5 %collective-permute-done.4 = f32[15,16,256]{2,1,0:T(8,128)S(1)} collective-permute-done((f32[15,16,256]{2,1,0:T(8,128)S(1)}, f32[15,16,256]{2,1,0:T(8,128)S(1)}, u32[]{:S(2)}, u32[]{:S(2)}) %collective-permute-start.4) | collective-permute-done | bytes 245792 | tf_op jit(solution)/shard_map/ppermute | solution.py:16
  118.0 2.9 %collective-permute-done.5 = f32[15,16,256]{2,1,0:T(8,128)S(1)} collective-permute-done((f32[15,16,256]{2,1,0:T(8,128)S(1)}, f32[15,16,256]{2,1,0:T(8,128)S(1)}, u32[]{:S(2)}, u32[]{:S(2)}) %collective-permute-start.5) | collective-permute-done | bytes 245792 | tf_op jit(solution)/shard_map/ppermute | solution.py:16
  121.1 0.1 fusion.82
  121.3 85.5 %all-to-all-done = f32[3,7,256,256]{3,1,0,2:T(8,128)} async-done(((f32[3,7,256,256]{3,1,0,2:T(8,128)}), f32[3,7,256,256]{3,1,0,2:T(8,128)}, u32[]{:S(2)}, u32[]{:S(2)}) %all-to-all-start) | async-done | bytes 5505056 | tf_op jit(solution)/shard_map/all_to_all | solution.py:11
  206.8 5.8 %fusion.7 = f32[3,7,16,256,1]{3,2,0,1,4:T(8,128)S(1)} fusion(f32[3,7,256,256,1]{3,1,0,2,4:T(8,128)} %bitcast.68, f32[3,7,16,7,256]{4,2,1,0,3:T(8,128)S(1)} %fusion.32), kind=kOutput, calls=%fused_computation.8 | convolution fusion | flops 924844032 | bytes 8257536 | tf_op jit(solution)/shard_map/ibcas,iasr->ibcr/dot_general | solution.py:70
  212.6 0.1 bitcast_multiply_fusion.1
  212.8 6.1 %collective-permute-start.6 = (f32[15,16,256]{2,1,0:T(8,128)S(1)}, f32[15,16,256]{2,1,0:T(8,128)S(1)}, u32[]{:S(2)}, u32[]{:S(2)}) collective-permute-start(f32[15,16,256]{2,1,0:T(8,128)S(1)} %pad_maximum_fusion.6), channel_id=1, source_target_pairs={{0,16},{16,32},{32,48},{48,64},{64,80},{80,96},{96,112},{112,128},... | collective-permute-start | bytes 737288 | tf_op jit(solution)/shard_map/ppermute | solution.py:16
  219.0 0.0 collective-permute-start.7
  219.0 3.1 %collective-permute-done.6 = f32[15,16,256]{2,1,0:T(8,128)S(1)} collective-permute-done((f32[15,16,256]{2,1,0:T(8,128)S(1)}, f32[15,16,256]{2,1,0:T(8,128)S(1)}, u32[]{:S(2)}, u32[]{:S(2)}) %collective-permute-start.6) | collective-permute-done | bytes 245792 | tf_op jit(solution)/shard_map/ppermute | solution.py:16
  222.3 0.1 bitcast_dynamic-update-slice_fusion.1
  222.4 2.2 collective-permute-done.7
  224.7 0.1 fusion.81
  224.9 6.1 %fusion.5 = f32[3,7,16,256,1]{3,2,0,1,4:T(8,128)S(1)} fusion(f32[3,7,256,256,1]{3,1,0,2,4:T(8,128)} %bitcast.68, f32[3,7,16,7,256]{4,2,1,0,3:T(8,128)S(1)} %fusion.20), kind=kOutput, calls=%fused_computation.6 | convolution fusion | flops 924844032 | bytes 8257536 | tf_op jit(solution)/shard_map/ibcas,iasr->ibcr/dot_general | solution.py:70
  230.9 0.9 fusion.78
  (101 shorter events, 1.6 us)
Async XLA Ops:
  6.5 82.2 %all-gather.2.cloned.1.call-start = ((), (), s32[]{:S(2)}) async-start(), calls=%async_computation.1 | async-start | bytes 5849088 | tf_op jit(solution)/shard_map/all_gather | solution.py:79
  9.1 8.9 %copy-start.1 = (pred[7]{0:T(512)(128)(4,1)S(1)}, pred[7]{0:T(512)(128)(4,1)}, u32[]{:S(2)}) copy-start(pred[7]{0:T(512)(128)(4,1)} %constant.7.clone.1) | copy-start | bytes 25
  9.2 7.9 %collective-permute-start = (f32[15,16,256]{2,1,0:T(8,128)S(1)}, f32[15,16,256]{2,1,0:T(8,128)S(1)}, u32[]{:S(2)}, u32[]{:S(2)}) collective-permute-start(f32[15,16,256]{2,1,0:T(8,128)S(1)} %pad_maximum_fusion), channel_id=1, source_target_pairs={{0,16},{16,32},{32,48},{48,64},{64,80},{80,96},{96,112},{112,128},... | collective-permute-start | bytes 737288 | tf_op jit(solution)/shard_map/ppermute | solution.py:16
  12.2 5.9 %copy-start = (f32[3,7,16,256]{3,2,1,0:T(8,128)S(1)}, f32[3,7,16,256]{3,2,1,0:T(8,128)}, u32[]{:S(2)}) copy-start(f32[3,7,16,256]{3,2,1,0:T(8,128)} %param.2) | copy-start | bytes 1032196
  12.2 5.6 %collective-permute-start.1 = (f32[15,16,256]{2,1,0:T(8,128)S(1)}, f32[15,16,256]{2,1,0:T(8,128)S(1)}, u32[]{:S(2)}, u32[]{:S(2)}) collective-permute-start(f32[15,16,256]{2,1,0:T(8,128)S(1)} %pad_maximum_fusion.1), channel_id=1, source_target_pairs={{0,496},{16,0},{32,16},{48,32},{64,48},{80,64},{96,80},{112,96},{1... | collective-permute-start | bytes 737288 | tf_op jit(solution)/shard_map/ppermute | solution.py:16
  88.7 12.4 %slice-start = ((s8[5505024]{0:T(1024)(128)(4,1)}), s8[4194304]{0:T(1024)(128)(4,1)S(1)}, s32[]{:S(2)}) async-start(s8[5505024]{0:T(1024)(128)(4,1)} %bitcast.251), calls=%async_computation.2 | async-start | bytes 8388608
  93.1 8.0 %slice-start.1 = ((s8[5505024]{0:T(1024)(128)(4,1)}), s8[1310720]{0:T(1024)(128)(4,1)S(1)}, s32[]{:S(2)}) async-start(s8[5505024]{0:T(1024)(128)(4,1)} %bitcast.251), calls=%async_computation.3 | async-start | bytes 2621440
  93.2 5.0 %collective-permute-start.2 = (f32[15,16,256]{2,1,0:T(8,128)S(1)}, f32[15,16,256]{2,1,0:T(8,128)S(1)}, u32[]{:S(2)}, u32[]{:S(2)}) collective-permute-start(f32[15,16,256]{2,1,0:T(8,128)S(1)} %pad_maximum_fusion.2), channel_id=1, source_target_pairs={{0,16},{16,32},{32,48},{48,64},{64,80},{80,96},{96,112},{112,128},... | collective-permute-start | bytes 737288 | tf_op jit(solution)/shard_map/ppermute | solution.py:16
  95.1 5.8 %collective-permute-start.3 = (f32[15,16,256]{2,1,0:T(8,128)S(1)}, f32[15,16,256]{2,1,0:T(8,128)S(1)}, u32[]{:S(2)}, u32[]{:S(2)}) collective-permute-start(f32[15,16,256]{2,1,0:T(8,128)S(1)} %pad_maximum_fusion.3), channel_id=1, source_target_pairs={{0,496},{16,0},{32,16},{48,32},{64,48},{80,64},{96,80},{112,96},{1... | collective-permute-start | bytes 737288 | tf_op jit(solution)/shard_map/ppermute | solution.py:16
  109.3 97.5 %all-to-all-start = ((f32[3,7,256,256]{3,1,0,2:T(8,128)}), f32[3,7,256,256]{3,1,0,2:T(8,128)}, u32[]{:S(2)}, u32[]{:S(2)}) async-start(f32[3,7,256,256]{3,1,0,2:T(8,128)} %copy.19), calls=%async_computation | async-start | bytes 12582912 | tf_op jit(solution)/shard_map/all_to_all | solution.py:11
  114.5 3.5 %collective-permute-start.4 = (f32[15,16,256]{2,1,0:T(8,128)S(1)}, f32[15,16,256]{2,1,0:T(8,128)S(1)}, u32[]{:S(2)}, u32[]{:S(2)}) collective-permute-start(f32[15,16,256]{2,1,0:T(8,128)S(1)} %pad_maximum_fusion.4), channel_id=1, source_target_pairs={{0,16},{16,32},{32,48},{48,64},{64,80},{80,96},{96,112},{112,128},... | collective-permute-start | bytes 737288 | tf_op jit(solution)/shard_map/ppermute | solution.py:16
  114.8 6.0 %collective-permute-start.5 = (f32[15,16,256]{2,1,0:T(8,128)S(1)}, f32[15,16,256]{2,1,0:T(8,128)S(1)}, u32[]{:S(2)}, u32[]{:S(2)}) collective-permute-start(f32[15,16,256]{2,1,0:T(8,128)S(1)} %pad_maximum_fusion.5), channel_id=1, source_target_pairs={{0,496},{16,0},{32,16},{48,32},{64,48},{80,64},{96,80},{112,96},{1... | collective-permute-start | bytes 737288 | tf_op jit(solution)/shard_map/ppermute | solution.py:16
  212.8 9.3 %collective-permute-start.6 = (f32[15,16,256]{2,1,0:T(8,128)S(1)}, f32[15,16,256]{2,1,0:T(8,128)S(1)}, u32[]{:S(2)}, u32[]{:S(2)}) collective-permute-start(f32[15,16,256]{2,1,0:T(8,128)S(1)} %pad_maximum_fusion.6), channel_id=1, source_target_pairs={{0,16},{16,32},{32,48},{48,64},{64,80},{80,96},{96,112},{112,128},... | collective-permute-start | bytes 737288 | tf_op jit(solution)/shard_map/ppermute | solution.py:16
  219.0 5.6 %collective-permute-start.7 = (f32[15,16,256]{2,1,0:T(8,128)S(1)}, f32[15,16,256]{2,1,0:T(8,128)S(1)}, u32[]{:S(2)}, u32[]{:S(2)}) collective-permute-start(f32[15,16,256]{2,1,0:T(8,128)S(1)} %pad_maximum_fusion.7), channel_id=1, source_target_pairs={{0,496},{16,0},{32,16},{48,32},{64,48},{80,64},{96,80},{112,96},{1... | collective-permute-start | bytes 737288 | tf_op jit(solution)/shard_map/ppermute | solution.py:16
Sparse Core Ops, SparseCore 0:
  10.4 78.2 all-gather.1
